TPU v7x, 256 devices: a whole 4x4x8 slice. The times are simulated.
256 devices in a mesh: expert: 32 (over x, z), tensor: 8 (over y, core).
Axes of the slice: x: 4, y: 4, z: 8, core: 2. Of those that a mesh axis runs over, the one named last changes fastest.
Arguments:
- attn_vals: bfloat16 [2048, 4096], P('expert', 'tensor'), may hold values from -6 to 6
- residual: bfloat16 [2048, 4096], P('expert', 'tensor'), may hold values from -6 to 6
- out_weight: bfloat16 [4096, 4096], P('tensor'), may hold values from -0.09375 to 0.09375
- norm_gain: float32 [4096], P('tensor'), may hold values from 0.5 to 1.5
- router_weight: float32 [4096, 8], P('tensor'), may hold values from -0.09375 to 0.09375
- routes: int32 [2048, 2], P('expert'), may hold values from 0 to 7, all different within a row; in each aligned block of 64 rows (0 to 63, 64 to 127, ...) at most 32 rows name the same one
- w_gate: bfloat16 [32, 4096, 2048], P('expert', None, 'tensor'), may hold values from -0.09375 to 0.09375
- w_up: bfloat16 [32, 4096, 2048], P('expert', None, 'tensor'), may hold values from -0.09375 to 0.09375
- w_down: bfloat16 [32, 2048, 4096], P('expert', 'tensor'), may hold values from -0.0625 to 0.0625
- slab_of: int32 [32], replicated, may hold values from 0 to 31, each once
- final_gain: float32 [4096], P('tensor'), may hold values from 0.5 to 1.5
- row_order: int32 [2048], replicated, may hold values from 0 to 2047, each once
Outputs:
- stream_out: bfloat16 [2048, 4096], P('expert', 'tensor')
- normed_out: bfloat16 [2048, 4096], P('expert', 'tensor')
Inputs may be any that keep to these rules, and one draw needn't show every extreme that they name: `routes`: the two experts of a row differ. In each aligned block of 64 rows (the rows of one device) no expert is named by more than 32 rows, and some block names one expert exactly 32 times. `slab_of`: A permutation. `row_order`: A permutation.
All inputs are finite; a program needn't handle non-finite values.
Results may differ from a plain program's by a relative error of at most 0.017.
Values may be sent and summed in bfloat16 or wider, within the bound.
No kernel may reach another device: no remote copies, remote signals or barrier semaphores. Data moves between devices by JAX's collectives and lax.ppermute only.
A program may use at most 128 MiB of HBM per device.

v0:
```python
import jax
import jax.numpy as jnp
from jax import lax
from jax.sharding import PartitionSpec as P

D = 4096
MOST = 32
EPS = 1e-05


def finish_slots(gate_val, up_val, down_weight):
    active = (jax.nn.silu(gate_val) * up_val).astype(jnp.bfloat16)
    partial_out = jnp.einsum("gmf,fd->gmd", active, down_weight, preferred_element_type=jnp.float32)
    summed = lax.psum_scatter(
        partial_out.astype(jnp.bfloat16), "tensor", scatter_dimension=2, tiled=True
    )
    return lax.all_to_all(summed, "expert", split_axis=0, concat_axis=0, tiled=True)


def final_norm(stream, final_gain):
    stream_f = stream.astype(jnp.float32)
    square_total = lax.psum(jnp.sum(stream_f * stream_f, axis=1), "tensor")
    factor = lax.rsqrt(square_total / D + EPS)
    return (stream_f * factor[:, None] * final_gain).astype(jnp.bfloat16)


def on_device(
    attn_vals,
    residual,
    out_weight,
    norm_gain,
    router_weight,
    routes,
    w_gate,
    w_up,
    w_down,
    slab_of,
    final_gain,
    row_order,
):
    groups = lax.axis_size("expert")
    row_count = attn_vals.shape[0]
    expert_count = router_weight.shape[1]
    slab_count = groups // expert_count
    partial_proj = jnp.dot(attn_vals, out_weight, preferred_element_type=jnp.float32)
    project = lax.psum_scatter(
        partial_proj.astype(jnp.bfloat16), "tensor", scatter_dimension=1, tiled=True
    ).astype(jnp.float32)
    stream_in = (residual.astype(jnp.float32) + project).astype(jnp.bfloat16)
    hidden_f = stream_in.astype(jnp.float32)
    scaled = hidden_f * norm_gain
    square_sum, logit_part = lax.psum(
        (
            jnp.sum(hidden_f * hidden_f, axis=1),
            jnp.dot(scaled, router_weight, precision=lax.Precision.HIGHEST),
        ),
        "tensor",
    )
    inverse_rms = lax.rsqrt(square_sum / D + EPS)
    normed_in = (scaled * inverse_rms[:, None]).astype(jnp.bfloat16)
    logits = logit_part * inverse_rms[:, None]
    expert_ids = jnp.arange(expert_count, dtype=jnp.int32)
    route_hot = (routes[:, :, None] == expert_ids[None, None, :]).astype(jnp.int32)
    chosen = jnp.sum(route_hot.astype(jnp.float32) * logits[:, None, :], axis=2)
    leading = jax.nn.sigmoid(chosen[:, 0] - chosen[:, 1])
    mixing = jnp.stack([leading, 1.0 - leading], axis=1)
    route_hits = jnp.sum(route_hot, axis=1)
    before_count = jnp.cumsum(route_hits, axis=0) - route_hits
    slot_ids = jnp.sum(route_hot * before_count[:, None, :], axis=2)
    slot_hot = (slot_ids[:, :, None] == jnp.arange(MOST, dtype=jnp.int32)[None, None, :]).astype(
        jnp.float32
    )
    placing = jnp.einsum("rke,rks->esr", route_hot.astype(jnp.float32), slot_hot).astype(
        jnp.bfloat16
    )
    target_expert = slab_of // slab_count
    send_map = jnp.take(placing, target_expert, axis=0)
    outgoing = jnp.einsum(
        "gsr,rd->gsd", send_map, normed_in, preferred_element_type=jnp.float32
    ).astype(jnp.bfloat16)
    arrived_part = lax.all_to_all(outgoing, "expert", split_axis=0, concat_axis=0, tiled=True)
    arrived = lax.all_gather(arrived_part, "tensor", axis=2, tiled=True)
    gate_val = jnp.einsum("gmd,df->gmf", arrived, w_gate[0], preferred_element_type=jnp.float32)
    up_val = jnp.einsum("gmd,df->gmf", arrived, w_up[0], preferred_element_type=jnp.float32)
    returned = finish_slots(gate_val, up_val, w_down[0])
    group_ids = jnp.arange(groups, dtype=jnp.int32)
    holder_hot = (slab_of[None, :] == group_ids[:, None]).astype(jnp.int32)
    holders = jnp.sum(holder_hot * group_ids[None, :], axis=1).reshape(expert_count, slab_count)
    row_holders = jnp.take(holders, routes, axis=0)
    flat_index = row_holders * MOST + slot_ids[:, :, None]
    flat_back = returned.reshape(groups * MOST, returned.shape[2])
    fetched = jnp.take(flat_back, flat_index.reshape(-1), axis=0).reshape(
        row_count, 2, slab_count, returned.shape[2]
    )
    expert_out = jnp.sum(fetched.astype(jnp.float32), axis=2)
    blended = jnp.sum(mixing[:, :, None] * expert_out, axis=1)
    stream = (hidden_f + blended).astype(jnp.bfloat16)
    positions = lax.axis_index("expert") * row_count + jnp.arange(row_count, dtype=jnp.int32)
    matches = (row_order[None, :] == positions[:, None]).astype(jnp.int32)
    source = jnp.sum(matches * jnp.arange(row_order.shape[0], dtype=jnp.int32)[None, :], axis=1)
    all_stream = lax.all_gather(stream, "expert", axis=0, tiled=True)
    ordered = jnp.take(all_stream, source, axis=0)
    return (ordered, final_norm(ordered, final_gain))


def solution(mesh):
    return jax.shard_map(
        on_device,
        mesh=mesh,
        in_specs=(
            P("expert", "tensor"),
            P("expert", "tensor"),
            P("tensor", None),
            P("tensor"),
            P("tensor", None),
            P("expert", None),
            P("expert", None, "tensor"),
            P("expert", None, "tensor"),
            P("expert", "tensor", None),
            P(),
            P("tensor"),
            P(),
        ),
        out_specs=(P("expert", "tensor"), P("expert", "tensor")),
        check_vma=False,
    )
```

profile of v0, /device:TPU:1, one launch (start us, length us, event | category | flops | bytes accessed | tf_op | source)
XLA Modules:
  0.0 367.0 jit_solution(5263027604369193061)
XLA Ops:
  7.2 0.0 copy-start
  7.2 0.0 copy-start.6
  7.2 0.0 reduce-scatter.3.cloned.1.call-start
  7.2 4.0 %convolution_convert_fusion.1 = bf16[64,4096]{1,0:T(8,128)(2,1)} fusion(bf16[64,512]{1,0:T(8,128)(2,1)} %param.12, bf16[512,4096]{1,0:T(8,128)(2,1)} %param.14), kind=kOutput, calls=%fused_computation.5 | convolution fusion | flops 268697600 | bytes 4784128 | tf_op jit(solution)/shard_map/dot_general | solution.py:45
  11.2 0.0 reduce-scatter.3.cloned.1.call-update
  11.3 0.0 all-gather.3.cloned.1.call-start
  11.3 0.0 copy-done.6
  11.3 0.1 copy.71
  11.4 0.2 convert_reduce_fusion.1
  11.6 0.1 reduce_window_sum.11
  11.7 1.2 select_reduce_fusion.1
  12.9 0.4 fusion.13
  13.4 0.1 copy.80
  13.5 0.0 copy-done.8
  13.6 0.6 gather_fusion.1
  14.2 32.7 %reduce-scatter.3.cloned.1.call-done = bf16[64,512]{1,0:T(8,128)(2,1)} async-done(((bf16[64,4096]{1,0:T(8,128)(2,1)}), bf16[64,512]{1,0:T(8,128)(2,1)}) %reduce-scatter.3.cloned.1.call-update) | async-done | bytes 65552 | tf_op jit(solution)/shard_map/reduce_scatter | solution.py:46
  46.8 0.0 copy-done.2
  46.8 1.0 fusion.28
  47.8 0.0 copy-done.3
  47.8 0.0 copy-done.4
  47.8 0.2 fusion.23
  48.0 14.9 %all-reduce = (f32[64]{0:T(128)S(1)}, f32[64,8]{0,1:T(8,128)S(1)}) all-reduce(f32[64]{0:T(128)S(1)} %get-tuple-element.10, f32[64,8]{0,1:T(8,128)S(1)} %fusion.23), channel_id=1, replica_groups=mesh['expert'=32,'tensor'=8] {'tensor'}, use_global_device_ids=true, to_apply=%region_4.0 | all-reduce | flops 576 | bytes 4608 | tf_op jit(solution)/shard_map/psum | solution.py:52
  62.9 0.5 convolution_convert_fusion.2
  63.4 34.6 %all_to_all.10 = bf16[32,32,512]{2,1,0:T(8,128)(2,1)} all-to-all(bf16[32,32,512]{2,1,0:T(8,128)(2,1)S(1)} %convolution_convert_fusion.2), channel_id=1, replica_groups=mesh['expert'=32,'tensor'=8] {'expert'}, dimensions={0} | all-to-all | bytes 2097152 | tf_op jit(solution)/shard_map/all_to_all | solution.py:81
  98.0 0.0 all-gather.3.cloned.1.call-update
  98.0 0.0 reduce-scatter.5.cloned.1.call-start
  98.1 50.6 %all-gather.3.cloned.1.call-done = bf16[32,32,4096]{2,1,0:T(8,128)(2,1)} async-done(((bf16[32,32,512]{2,1,0:T(8,128)(2,1)}), bf16[32,32,4096]{2,1,0:T(8,128)(2,1)}) %all-gather.3.cloned.1.call-update) | async-done | bytes 8388624 | tf_op jit(solution)/shard_map/all_gather | solution.py:82
  148.7 6.3 %fusion.3 = f32[32,32,256]{2,1,0:T(8,128)S(1)} fusion(bf16[32,32,4096]{2,1,0:T(8,128)(2,1)} %all-gather.3.cloned.1.call-done, bf16[1,4096,256]{2,1,0:T(8,128)(2,1)} %param.18), kind=kOutput, calls=%fused_computation.9 | convolution fusion | flops 2147483648 | bytes 11534336 | tf_op jit(solution)/shard_map/gmd,df->gmf/dot_general | solution.py:83
  155.0 0.0 copy-done
  155.0 16.8 %convolution_convert_fusion = bf16[32,32,4096]{2,1,0:T(8,128)(2,1)} fusion(bf16[1,256,4096]{2,1,0:T(8,128)(2,1)S(1)} %copy-done, bf16[32,32,4096]{2,1,0:T(8,128)(2,1)} %all-gather.3.cloned.1.call-done, bf16[1,4096,256]{2,1,0:T(8,128)(2,1)} %param.19, f32[32,32,256]{2,1,0:T(8,128)S(1)} %fusion.3), kind=kOutput, calls=%fused_computation.4 | convolution fusion | flops 4300734464 | bytes 22020096 | tf_op jit(solution)/shard_map/gmf,fd->gmd/dot_general | solution.py:13
  171.8 0.0 reduce-scatter.5.cloned.1.call-update
  171.8 54.4 %reduce-scatter.5.cloned.1.call-done = bf16[32,32,512]{2,1,0:T(8,128)(2,1)} async-done(((bf16[32,32,4096]{2,1,0:T(8,128)(2,1)}), bf16[32,32,512]{2,1,0:T(8,128)(2,1)}) %reduce-scatter.5.cloned.1.call-update) | async-done | bytes 1048592 | tf_op jit(solution)/shard_map/reduce_scatter | solution.py:14
  226.2 9.5 %all-to-all-start.1 = ((bf16[32,32,512]{2,1,0:T(8,128)(2,1)}), bf16[32,32,512]{2,1,0:T(8,128)(2,1)S(1)}, u32[]{:S(2)}, u32[]{:S(2)}) async-start(bf16[32,32,512]{2,1,0:T(8,128)(2,1)} %reduce-scatter.5.cloned.1.call-done), calls=%async_computation.3 | async-start | bytes 2097152 | tf_op jit(solution)/shard_map/all_to_all | solution.py:17
  235.8 0.2 all-gather.5.cloned.1.call-start
  236.0 0.1 copy.78
  236.1 0.1 copy.76
  236.2 0.1 reshape.129
  236.3 0.1 select_reduce_fusion.2
  236.5 0.1 reshape.125
  236.6 0.6 gather_fusion
  237.2 0.1 copy.77
  237.3 0.1 copy.81
  237.4 0.1 add.139
  237.6 0.1 copy.79
  237.8 0.1 copy.72
  237.9 0.2 fusion.33
  238.1 0.1 fusion.45
  238.2 0.1 copy.84
  238.2 0.1 copy.85
  238.4 0.1 copy.75
  238.4 22.5 %all-to-all-done.1 = bf16[32,32,512]{2,1,0:T(8,128)(2,1)S(1)} async-done(((bf16[32,32,512]{2,1,0:T(8,128)(2,1)}), bf16[32,32,512]{2,1,0:T(8,128)(2,1)S(1)}, u32[]{:S(2)}, u32[]{:S(2)}) %all-to-all-start.1) | async-done | bytes 1048608 | tf_op jit(solution)/shard_map/all_to_all | solution.py:17
  261.0 2.6 gather_fusion.2
  263.6 1.2 gather.21
  264.8 0.9 convert_reduce_fusion
  265.7 0.4 multiply_reduce_fusion
  266.1 0.6 fusion.29
  266.8 0.0 all-gather.5.cloned.1.call-update
  266.8 0.2 select_reduce_fusion
  267.1 72.8 %all-gather.5.cloned.1.call-done = bf16[2048,512]{1,0:T(8,128)(2,1)} async-done(((bf16[64,512]{1,0:T(8,128)(2,1)}), bf16[2048,512]{1,0:T(8,128)(2,1)}) %all-gather.5.cloned.1.call-update) | async-done | bytes 2097168 | tf_op jit(solution)/shard_map/all_gather | solution.py:101
  339.9 2.6 gather_fusion.3
  342.5 0.2 fusion.25
  342.6 0.0 copy-start.1
  342.7 17.1 %psum.23 = f32[64]{0:T(128)S(1)} all-reduce(f32[64]{0:T(128)S(1)} %get-tuple-element.4), channel_id=1, replica_groups=mesh['expert'=32,'tensor'=8] {'tensor'}, use_global_device_ids=true, to_apply=%region_14.15 | all-reduce | flops 64 | bytes 512 | tf_op jit(solution)/shard_map/psum | solution.py:22
  359.7 0.7 fusion.27
  (27 shorter events, 0.2 us)
Async XLA Ops:
  7.2 147.8 %copy-start = (bf16[1,256,4096]{2,1,0:T(8,128)(2,1)S(1)}, bf16[1,256,4096]{2,1,0:T(8,128)(2,1)}, u32[]{:S(2)}) copy-start(bf16[1,256,4096]{2,1,0:T(8,128)(2,1)} %param.20) | copy-start | bytes 6291460
  7.2 4.1 %copy-start.6 = (s32[64,2]{0,1:T(2,128)S(1)}, s32[64,2]{0,1:T(2,128)}, u32[]{:S(2)}) copy-start(s32[64,2]{0,1:T(2,128)} %param.17) | copy-start | bytes 1540
  7.2 39.6 %reduce-scatter.3.cloned.1.call-start = ((), (), s32[]{:S(2)}) async-start(), calls=%async_computation.4 | async-start | bytes 589824 | tf_op jit(solution)/shard_map/reduce_scatter | solution.py:46
  11.2 2.3 copy-start.8
  11.2 35.6 %copy-start.2 = (bf16[64,512]{1,0:T(8,128)(2,1)S(1)}, bf16[64,512]{1,0:T(8,128)(2,1)}, u32[]{:S(2)}) copy-start(bf16[64,512]{1,0:T(8,128)(2,1)} %param.13) | copy-start | bytes 196612
  11.2 36.6 %copy-start.3 = (f32[512,8]{0,1:T(8,128)S(1)}, f32[512,8]{0,1:T(8,128)}, u32[]{:S(2)}) copy-start(f32[512,8]{0,1:T(8,128)} %param.16) | copy-start | bytes 49156
  11.2 36.6 %copy-start.4 = (f32[512]{0:T(512)S(1)}, f32[512]{0:T(512)}, u32[]{:S(2)}) copy-start(f32[512]{0:T(512)} %param.15) | copy-start | bytes 6148
  11.3 137.4 %all-gather.3.cloned.1.call-start = ((), (), s32[]{:S(2)}) async-start(), calls=%async_computation.5 | async-start | bytes 9437184 | tf_op jit(solution)/shard_map/all_gather | solution.py:82
  98.0 128.2 %reduce-scatter.5.cloned.1.call-start = ((), (), s32[]{:S(2)}) async-start(), calls=%async_computation.6 | async-start | bytes 9437184 | tf_op jit(solution)/shard_map/reduce_scatter | solution.py:14
  226.2 34.7 %all-to-all-start.1 = ((bf16[32,32,512]{2,1,0:T(8,128)(2,1)}), bf16[32,32,512]{2,1,0:T(8,128)(2,1)S(1)}, u32[]{:S(2)}, u32[]{:S(2)}) async-start(bf16[32,32,512]{2,1,0:T(8,128)(2,1)} %reduce-scatter.5.cloned.1.call-done), calls=%async_computation.3 | async-start | bytes 2097152 | tf_op jit(solution)/shard_map/all_to_all | solution.py:17
  235.8 104.1 %all-gather.5.cloned.1.call-start = ((), (), s32[]{:S(2)}) async-start(), calls=%async_computation.7 | async-start | bytes 2162688 | tf_op jit(solution)/shard_map/all_gather | solution.py:101
  263.6 3.2 copy-start.5
  263.6 96.2 %copy-start.7 = (f32[512]{0:T(512)S(1)}, f32[512]{0:T(512)}, u32[]{:S(2)}) copy-start(f32[512]{0:T(512)} %param.22) | copy-start | bytes 6148
  342.6 17.8 %copy-start.1 = (bf16[64,512]{1,0:T(8,128)(2,1)}, bf16[64,512]{1,0:T(8,128)(2,1)S(1)}, u32[]{:S(2)}) copy-start(bf16[64,512]{1,0:T(8,128)(2,1)S(1)} %get-tuple-element.5) | copy-start | bytes 196612
Sparse Core Ops, SparseCore 0:
  11.4 35.4 reduce-scatter.2
  98.1 50.5 all-gather.2
  172.0 54.2 reduce-scatter.4
  266.9 72.9 all-gather.4
where the time goes:
time: 367 us
  waiting for transfers between devices  233 us (63%)
  blocking collectives  66.5 us (18%)
  matrix products  28.2 us (8%)
  between operations  14.1 us (4%)
  starting transfers between devices  9.88 us (3%)
  local copies, waits for them, and re-layouts  9.17 us (2%)
  other arithmetic  6.03 us (2%)
    all_gather x1, waiting for transfers between devices, on_device(): all_stream = lax.all_gather(stream, 'expert', axis=0, tiled=True)  72.8 us
    reduce_scatter x1, waiting for transfers between devices, finish_slots(): lax.psum_scatter(partial_out.astype(jnp.bfloat16), 'tensor', scatter_dime...  54.4 us
    all_gather x1, waiting for transfers between devices, on_device(): arrived = lax.all_gather(arrived_part, 'tensor', axis=2, tiled=True)  50.6 us
    all_to_all x1, blocking collectives, on_device(): lax.all_to_all(outgoing, 'expert', split_axis=0, concat_axis=0, tiled=True)  34.6 us
    reduce_scatter x1, waiting for transfers between devices, on_device(): lax.psum_scatter(partial_proj.astype(jnp.bfloat16), 'tensor', scatter_dim...  32.7 us
    all_to_all x1, waiting for transfers between devices, finish_slots(): lax.all_to_all(summed, 'expert', split_axis=0, concat_axis=0, tiled=True)  22.5 us
    psum x1, blocking collectives, final_norm(): square_total = lax.psum(jnp.sum(stream_f * stream_f, axis=1), 'tensor')  17.1 us
    dot_general x1, matrix products, finish_slots(): jnp.einsum('gmf,fd->gmd', active, down_weight, preferred_element_type=jnp...  16.8 us
  transfers between devices with their start and end apart: 5, of which 5 were waited for; matrix products, arithmetic and copies ran while one was open for 1% of the time, Pallas kernels for 0%

commit v1 on v0

--- a/solution.py
+++ b/solution.py
@@ -19,7 +19,9 @@
 
 def final_norm(stream, final_gain):
     stream_f = stream.astype(jnp.float32)
-    square_total = lax.psum(jnp.sum(stream_f * stream_f, axis=1), "tensor")
+    square_total = jax.lax.all_gather(jnp.sum(stream_f * stream_f, axis=1), axis_name="tensor").sum(
+        axis=0
+    )
     factor = lax.rsqrt(square_total / D + EPS)
     return (stream_f * factor[:, None] * final_gain).astype(jnp.bfloat16)
 

time: 367 us -> 368 us (level)
    psum x1 -> x0, blocking collectives: 17.1 us -> none  [final_norm(): square_total = lax.psum(jnp.sum(stream_f * stream_f, axis=1), 'tensor')]
    unnamed x0 -> x1, blocking collectives: none -> 17.1 us
  transfers between devices with their start and end apart: 5 -> 5, of which waited for: 5 -> 5; matrix products, arithmetic and copies ran while one was open for 1% -> 2% of each run, Pallas kernels for 0% -> 0%
where the time goes in v1:
time: 368 us; the launch traced here: 367 us
  waiting for transfers between devices  232 us (63%)
  blocking collectives  66.5 us (18%)
  matrix products  28.2 us (8%)
  between operations  14.7 us (4%)
  local copies, waits for them, and re-layouts  10.1 us (3%)
  starting transfers between devices  9.88 us (3%)
  other arithmetic  6.05 us (2%)
    all_gather x1, waiting for transfers between devices, on_device(): all_stream = lax.all_gather(stream, 'expert', axis=0, tiled=True)  71.6 us
    reduce_scatter x1, waiting for transfers between devices, finish_slots(): lax.psum_scatter(partial_out.astype(jnp.bfloat16), 'tensor', scatter_dime...  54.4 us
    all_gather x1, waiting for transfers between devices, on_device(): arrived = lax.all_gather(arrived_part, 'tensor', axis=2, tiled=True)  50.6 us
    all_to_all x1, blocking collectives, on_device(): lax.all_to_all(outgoing, 'expert', split_axis=0, concat_axis=0, tiled=True)  34.6 us
    reduce_scatter x1, waiting for transfers between devices, on_device(): lax.psum_scatter(partial_proj.astype(jnp.bfloat16), 'tensor', scatter_dim...  32.7 us
    all_to_all x1, waiting for transfers between devices, finish_slots(): lax.all_to_all(summed, 'expert', split_axis=0, concat_axis=0, tiled=True)  22.5 us
    unnamed x1, blocking collectives  17.1 us
    dot_general x1, matrix products, finish_slots(): jnp.einsum('gmf,fd->gmd', active, down_weight, preferred_element_type=jnp...  16.8 us
  transfers between devices with their start and end apart: 5, of which 5 were waited for; matrix products, arithmetic and copies ran while one was open for 2% of the time, Pallas kernels for 0%

profile of v1, /device:TPU:1, one launch (start us, length us, event | category | flops | bytes accessed | tf_op | source)
XLA Modules:
  0.0 367.4 jit_solution(320725291776440441)
XLA Ops:
  7.2 0.0 copy-start
  7.2 0.0 copy-start.6
  7.2 0.0 reduce-scatter.3.cloned.1.call-start
  7.2 4.0 %convolution_convert_fusion.1 = bf16[64,4096]{1,0:T(8,128)(2,1)} fusion(bf16[64,512]{1,0:T(8,128)(2,1)} %param.12, bf16[512,4096]{1,0:T(8,128)(2,1)} %param.14), kind=kOutput, calls=%fused_computation.5 | convolution fusion | flops 268697600 | bytes 4784128 | tf_op jit(solution)/shard_map/dot_general | solution.py:47
  11.2 0.0 reduce-scatter.3.cloned.1.call-update
  11.3 0.0 all-gather.4.cloned.1.call-start
  11.3 0.0 copy-done.6
  11.3 0.1 copy.71
  11.4 0.2 convert_reduce_fusion.1
  11.6 0.1 reduce_window_sum.11
  11.7 1.2 select_reduce_fusion.1
  12.9 0.4 fusion.13
  13.4 0.1 copy.80
  13.5 0.0 copy-done.8
  13.6 0.6 gather_fusion.1
  14.2 32.7 %reduce-scatter.3.cloned.1.call-done = bf16[64,512]{1,0:T(8,128)(2,1)} async-done(((bf16[64,4096]{1,0:T(8,128)(2,1)}), bf16[64,512]{1,0:T(8,128)(2,1)}) %reduce-scatter.3.cloned.1.call-update) | async-done | bytes 65552 | tf_op jit(solution)/shard_map/reduce_scatter | solution.py:48
  46.8 1.0 fusion.28
  47.8 0.2 fusion.23
  48.0 14.9 %all-reduce.1 = (f32[64]{0:T(128)S(1)}, f32[64,8]{0,1:T(8,128)S(1)}) all-reduce(f32[64]{0:T(128)S(1)} %get-tuple-element.10, f32[64,8]{0,1:T(8,128)S(1)} %fusion.23), channel_id=1, replica_groups=mesh['expert'=32,'tensor'=8] {'tensor'}, use_global_device_ids=true, to_apply=%region_4.0 | all-reduce | flops 576 | bytes 4608 | tf_op jit(solution)/shard_map/psum | solution.py:54
  62.9 0.5 convolution_convert_fusion.2
  63.4 34.6 %all_to_all.10 = bf16[32,32,512]{2,1,0:T(8,128)(2,1)} all-to-all(bf16[32,32,512]{2,1,0:T(8,128)(2,1)S(1)} %convolution_convert_fusion.2), channel_id=1, replica_groups=mesh['expert'=32,'tensor'=8] {'expert'}, dimensions={0} | all-to-all | bytes 2097152 | tf_op jit(solution)/shard_map/all_to_all | solution.py:83
  98.0 0.0 all-gather.4.cloned.1.call-update
  98.0 0.0 reduce-scatter.5.cloned.1.call-start
  98.1 50.6 %all-gather.4.cloned.1.call-done = bf16[32,32,4096]{2,1,0:T(8,128)(2,1)} async-done(((bf16[32,32,512]{2,1,0:T(8,128)(2,1)}), bf16[32,32,4096]{2,1,0:T(8,128)(2,1)}) %all-gather.4.cloned.1.call-update) | async-done | bytes 8388624 | tf_op jit(solution)/shard_map/all_gather | solution.py:84
  148.7 6.3 %fusion.3 = f32[32,32,256]{2,1,0:T(8,128)S(1)} fusion(bf16[32,32,4096]{2,1,0:T(8,128)(2,1)} %all-gather.4.cloned.1.call-done, bf16[1,4096,256]{2,1,0:T(8,128)(2,1)} %param.18), kind=kOutput, calls=%fused_computation.9 | convolution fusion | flops 2147483648 | bytes 11534336 | tf_op jit(solution)/shard_map/gmd,df->gmf/dot_general | solution.py:85
  155.0 16.8 %convolution_convert_fusion = bf16[32,32,4096]{2,1,0:T(8,128)(2,1)} fusion(bf16[1,256,4096]{2,1,0:T(8,128)(2,1)S(1)} %copy-done, bf16[32,32,4096]{2,1,0:T(8,128)(2,1)} %all-gather.4.cloned.1.call-done, bf16[1,4096,256]{2,1,0:T(8,128)(2,1)} %param.19, f32[32,32,256]{2,1,0:T(8,128)S(1)} %fusion.3), kind=kOutput, calls=%fused_computation.4 | convolution fusion | flops 4300734464 | bytes 22020096 | tf_op jit(solution)/shard_map/gmf,fd->gmd/dot_general | solution.py:13
  171.8 0.0 reduce-scatter.5.cloned.1.call-update
  171.8 54.4 %reduce-scatter.5.cloned.1.call-done = bf16[32,32,512]{2,1,0:T(8,128)(2,1)} async-done(((bf16[32,32,4096]{2,1,0:T(8,128)(2,1)}), bf16[32,32,512]{2,1,0:T(8,128)(2,1)}) %reduce-scatter.5.cloned.1.call-update) | async-done | bytes 1048592 | tf_op jit(solution)/shard_map/reduce_scatter | solution.py:14
  226.2 9.5 %all-to-all-start.1 = ((bf16[32,32,512]{2,1,0:T(8,128)(2,1)}), bf16[32,32,512]{2,1,0:T(8,128)(2,1)S(1)}, u32[]{:S(2)}, u32[]{:S(2)}) async-start(bf16[32,32,512]{2,1,0:T(8,128)(2,1)} %reduce-scatter.5.cloned.1.call-done), calls=%async_computation.3 | async-start | bytes 2097152 | tf_op jit(solution)/shard_map/all_to_all | solution.py:17
  235.8 0.2 all-gather.6.cloned.1.call-start
  236.0 0.1 copy.78
  236.1 0.1 copy.76
  236.2 0.1 reshape.133
  236.3 0.1 select_reduce_fusion.2
  236.5 0.1 reshape.129
  236.6 0.6 gather_fusion
  237.2 0.1 copy.77
  237.3 0.1 copy.81
  237.4 0.1 add.141
  237.6 0.1 copy.79
  237.8 0.1 copy.72
  237.9 0.2 fusion.33
  238.1 0.1 fusion.45
  238.2 0.1 copy.84
  238.2 0.1 copy.85
  238.4 0.1 copy.75
  238.4 22.5 %all-to-all-done.1 = bf16[32,32,512]{2,1,0:T(8,128)(2,1)S(1)} async-done(((bf16[32,32,512]{2,1,0:T(8,128)(2,1)}), bf16[32,32,512]{2,1,0:T(8,128)(2,1)S(1)}, u32[]{:S(2)}, u32[]{:S(2)}) %all-to-all-start.1) | async-done | bytes 1048608 | tf_op jit(solution)/shard_map/all_to_all | solution.py:17
  261.0 2.6 gather_fusion.2
  263.6 1.2 gather.21
  264.8 0.9 convert_reduce_fusion
  265.7 0.4 multiply_reduce_fusion
  266.1 0.6 fusion.29
  266.8 0.0 all-gather.6.cloned.1.call-update
  266.8 0.6 dynamic-slice
  268.1 0.0 copy-done.5
  268.1 0.2 select_reduce_fusion
  268.3 71.6 %all-gather.6.cloned.1.call-done = bf16[2048,512]{1,0:T(8,128)(2,1)} async-done(((bf16[64,512]{1,0:T(8,128)(2,1)}), bf16[2048,512]{1,0:T(8,128)(2,1)}) %all-gather.6.cloned.1.call-update) | async-done | bytes 2097168 | tf_op jit(solution)/shard_map/all_gather | solution.py:103
  339.9 2.6 gather_fusion.3
  342.5 0.2 fusion.25
  342.7 0.0 copy-start.1
  342.7 0.2 dynamic-update-slice
  343.0 17.1 %all-reduce = f32[512]{0:T(512)S(1)} all-reduce(f32[512]{0:T(512)S(1)} %dynamic-update-slice), channel_id=2, replica_groups=mesh['expert'=32,'tensor'=8] {'tensor'}, use_global_device_ids=true, to_apply=%add | all-reduce | flops 512 | bytes 4096
  360.0 0.1 reshape.163
  360.1 0.7 fusion.27
  (34 shorter events, 0.2 us)
Async XLA Ops:
  7.2 147.8 %copy-start = (bf16[1,256,4096]{2,1,0:T(8,128)(2,1)S(1)}, bf16[1,256,4096]{2,1,0:T(8,128)(2,1)}, u32[]{:S(2)}) copy-start(bf16[1,256,4096]{2,1,0:T(8,128)(2,1)} %param.20) | copy-start | bytes 6291460
  7.2 4.1 %copy-start.6 = (s32[64,2]{0,1:T(2,128)S(1)}, s32[64,2]{0,1:T(2,128)}, u32[]{:S(2)}) copy-start(s32[64,2]{0,1:T(2,128)} %param.17) | copy-start | bytes 1540
  7.2 39.6 %reduce-scatter.3.cloned.1.call-start = ((), (), s32[]{:S(2)}) async-start(), calls=%async_computation.4 | async-start | bytes 589824 | tf_op jit(solution)/shard_map/reduce_scatter | solution.py:48
  11.2 2.3 copy-start.8
  11.2 35.6 %copy-start.2 = (bf16[64,512]{1,0:T(8,128)(2,1)S(1)}, bf16[64,512]{1,0:T(8,128)(2,1)}, u32[]{:S(2)}) copy-start(bf16[64,512]{1,0:T(8,128)(2,1)} %param.13) | copy-start | bytes 196612
  11.2 36.6 %copy-start.3 = (f32[512,8]{0,1:T(8,128)S(1)}, f32[512,8]{0,1:T(8,128)}, u32[]{:S(2)}) copy-start(f32[512,8]{0,1:T(8,128)} %param.16) | copy-start | bytes 49156
  11.2 36.6 %copy-start.4 = (f32[512]{0:T(512)S(1)}, f32[512]{0:T(512)}, u32[]{:S(2)}) copy-start(f32[512]{0:T(512)} %param.15) | copy-start | bytes 6148
  11.3 137.4 %all-gather.4.cloned.1.call-start = ((), (), s32[]{:S(2)}) async-start(), calls=%async_computation.5 | async-start | bytes 9437184 | tf_op jit(solution)/shard_map/all_gather | solution.py:84
  98.0 128.2 %reduce-scatter.5.cloned.1.call-start = ((), (), s32[]{:S(2)}) async-start(), calls=%async_computation.6 | async-start | bytes 9437184 | tf_op jit(solution)/shard_map/reduce_scatter | solution.py:14
  226.2 34.7 %all-to-all-start.1 = ((bf16[32,32,512]{2,1,0:T(8,128)(2,1)}), bf16[32,32,512]{2,1,0:T(8,128)(2,1)S(1)}, u32[]{:S(2)}, u32[]{:S(2)}) async-start(bf16[32,32,512]{2,1,0:T(8,128)(2,1)} %reduce-scatter.5.cloned.1.call-done), calls=%async_computation.3 | async-start | bytes 2097152 | tf_op jit(solution)/shard_map/all_to_all | solution.py:17
  235.8 104.1 %all-gather.6.cloned.1.call-start = ((), (), s32[]{:S(2)}) async-start(), calls=%async_computation.7 | async-start | bytes 2162688 | tf_op jit(solution)/shard_map/all_gather | solution.py:103
  263.6 3.2 copy-start.9
  263.6 4.5 %copy-start.5 = (s32[2048]{0:T(1024)S(1)}, s32[2048]{0:T(1024)}, u32[]{:S(2)}) copy-start(s32[2048]{0:T(1024)} %param.23) | copy-start | bytes 24580
  263.6 96.5 %copy-start.7 = (f32[512]{0:T(512)S(1)}, f32[512]{0:T(512)}, u32[]{:S(2)}) copy-start(f32[512]{0:T(512)} %param.22) | copy-start | bytes 6148
  342.7 18.2 %copy-start.1 = (bf16[64,512]{1,0:T(8,128)(2,1)}, bf16[64,512]{1,0:T(8,128)(2,1)S(1)}, u32[]{:S(2)}) copy-start(bf16[64,512]{1,0:T(8,128)(2,1)S(1)} %get-tuple-element.5) | copy-start | bytes 196612
Sparse Core Ops, SparseCore 0:
  11.4 35.4 reduce-scatter.2
  98.1 50.5 all-gather.3
  172.0 54.2 reduce-scatter.4
  266.9 72.9 all-gather.5
